TPU v7x, 512 devices: a whole 4x4x16 slice. The times are simulated.
512 devices in a mesh: ops: 16 (over x, y), sec: 32 (over z, core).
Axes of the slice: x: 4, y: 4, z: 16, core: 2. Of those that a mesh axis runs over, the one named last changes fastest.
Arguments:
- wave: bfloat16 [32, 768, 768], P('sec')
- left_ops: bfloat16 [16, 32, 768, 768], P('ops', 'sec'), may hold values from -0.21875 to 0.21875
- right_ops: bfloat16 [16, 32, 768, 768], P('ops', 'sec'), may hold values from -0.21875 to 0.21875
- priors: bfloat16 [8, 32, 768, 768], P(None, 'sec', 'ops'), as said below
- row_sizes: int32 [32], P('sec'), may hold values from 64 to 768, as said below
- col_sizes: int32 [32], P('sec'), may hold values from 64 to 768, as said below
Outputs:
- sigma: bfloat16 [32, 768, 768], P('sec', 'ops')
- new_dir: bfloat16 [32, 768, 768], P('sec', 'ops')
- correlations: float32 [8], replicated
Inputs may be any that keep to these rules, and one draw needn't show every extreme that they name: `row_sizes`: one sector's block uses all 768 rows. `col_sizes`: one sector's block uses all 768 columns. `priors`: each prior vector has a norm of about one over all cells.
All inputs are finite; a program needn't handle non-finite values.
Results may differ from a plain program's by a relative error of at most 0.012.
Values sent between devices are 32-bit elements; how exact they have to be, the bound alone decides.
No kernel may reach another device: no remote copies, remote signals or barrier semaphores. Data moves between devices by JAX's collectives and lax.ppermute only.
A program may use at most 64 MiB of HBM per device.

v0:
```python
import jax
import jax.numpy as jnp
from jax import lax
from jax.sharding import PartitionSpec as P


def shards(wave, left_ops, right_ops, priors, row_sizes, col_sizes):
    width = wave.shape[1]
    sec_local = wave.shape[0]
    shard_rows = width // lax.axis_size("ops")
    first_row = lax.axis_index("ops") * shard_rows
    place = jnp.arange(width, dtype=jnp.int32)
    row_mask = (place[None, :] < row_sizes[:, None]).astype(jnp.float32)
    col_mask = (place[None, :] < col_sizes[:, None]).astype(jnp.float32)
    full_mask = row_mask[:, :, None] * col_mask[:, None, :]
    masked = wave * full_mask.astype(jnp.bfloat16)
    inner = jnp.einsum(
        "sab,ksjb->ksaj", masked, right_ops, preferred_element_type=jnp.float32
    ).astype(jnp.bfloat16)
    partial_all = jnp.einsum("ksia,ksaj->sij", left_ops, inner, preferred_element_type=jnp.float32)
    whole = lax.psum(partial_all, "ops")
    summed = lax.dynamic_slice_in_dim(whole, first_row, shard_rows, 1)
    mine_rows = lax.dynamic_slice_in_dim(row_mask, first_row, shard_rows, 1)
    mine_mask = mine_rows[:, :, None] * col_mask[:, None, :]
    sigma = (summed * mine_mask).astype(jnp.bfloat16)
    pmask = (priors * mine_mask[None].astype(jnp.bfloat16)).astype(jnp.float32)
    sig32 = sigma.astype(jnp.float32)
    local_over = jnp.einsum("psab,sab->p", pmask, sig32, precision=lax.Precision.HIGHEST)
    correlations = lax.psum(local_over, ("ops", "sec"))
    resid = sig32 - jnp.einsum("p,psab->sab", correlations, pmask, precision=lax.Precision.HIGHEST)
    total = lax.psum(jnp.sum(resid * resid), ("ops", "sec"))
    cells = sec_local * lax.axis_size("sec") * width * width
    new_dir = (resid / jnp.sqrt(total / cells + 1e-06)).astype(jnp.bfloat16)
    return (sigma, new_dir, correlations)


def solution(mesh):
    in_specs = (
        P("sec", None, None),
        P("ops", "sec", None, None),
        P("ops", "sec", None, None),
        P(None, "sec", "ops", None),
        P("sec"),
        P("sec"),
    )
    out_specs = (P("sec", "ops", None), P("sec", "ops", None), P())
    return jax.shard_map(shards, mesh=mesh, in_specs=in_specs, out_specs=out_specs, check_vma=False)
```

profile of v0, /device:TPU:1, one launch (start us, length us, event | category | flops | bytes accessed | tf_op | source)
XLA Modules:
  0.0 362.4 jit_solution(13174631265643082113)
XLA Ops:
  7.2 0.0 copy-start
  7.2 0.0 all-reduce.2.cloned.1.call-start
  8.6 0.0 copy-done
  8.6 5.6 %convolution_bitcast_fusion = f32[1,768,768]{1,2,0:T(8,128)} fusion(bf16[1,1,768,768]{3,2,1,0:T(8,128)(2,1)S(1)} %copy-done, bf16[1,768,768]{2,1,0:T(8,128)(2,1)} %param.6, bf16[1,1,768,768]{3,2,1,0:T(8,128)(2,1)} %param.8, f32[768]{0:T(1024)S(1)} %get-tuple-element.7, f32[768]{0:T(1024)S(1)} %get-tuple-element.6), kind=kOutput, calls=%fused_computation.1 | convolution fusion | flops 1814298624 | bytes 5904384 | tf_op jit(solution)/shard_map/ksia,ksaj->sij/dot_general | solution.py:20
  14.2 0.0 copy-start.1
  14.2 0.0 all-reduce.2.cloned.1.call-update
  14.2 0.1 multiply_convert_fusion.2
  14.3 0.9 copy-done.1
  15.3 125.8 %all-reduce.2.cloned.1.call-done = f32[1,768,768]{1,2,0:T(8,128)} async-done(((f32[1,768,768]{1,2,0:T(8,128)}), f32[1,768,768]{1,2,0:T(8,128)}) %all-reduce.2.cloned.1.call-update) | async-done | bytes 2359312 | tf_op jit(solution)/shard_map/psum | solution.py:21
  141.1 1.4 fusion.19
  142.5 0.2 copy.12
  142.7 0.5 convolution_bitcast_fusion.1
  143.2 105.0 %psum.22 = f32[8]{0:T(128)S(1)} all-reduce(f32[8]{0:T(128)S(1)} %convolution_bitcast_fusion.1), channel_id=1, replica_groups=mesh['ops'=16,'sec'=32] {'ops','sec'}, use_global_device_ids=true, to_apply=%region_1.0 | all-reduce | flops 8 | bytes 64 | tf_op jit(solution)/shard_map/psum | solution.py:29
  248.2 0.0 copy-start.2
  248.2 0.6 fusion.11
  248.8 0.2 copy.13
  249.0 1.4 multiply_convert_fusion.1
  250.4 2.0 multiply_reduce_fusion
  252.4 0.0 copy-done.2
  252.4 0.8 copy.9
  253.2 99.5 %psum.23 = f32[]{:T(128)} all-reduce(f32[]{:T(128)} %multiply_reduce_fusion), channel_id=1, replica_groups=mesh['ops'=16,'sec'=32] {'ops','sec'}, use_global_device_ids=true, to_apply=%region_3.0 | all-reduce | flops 1 | bytes 8 | tf_op jit(solution)/shard_map/psum | solution.py:31
  353.4 1.4 divide_convert_fusion
  354.8 0.8 copy.10
  (3 shorter events, 0.1 us)
Async XLA Ops:
  7.2 1.5 copy-start
  7.2 133.9 %all-reduce.2.cloned.1.call-start = ((), (), s32[]{:S(2)}) async-start(), calls=%async_computation | async-start | bytes 4718592 | tf_op jit(solution)/shard_map/psum | solution.py:21
  14.2 1.1 copy-start.1
  248.2 4.3 %copy-start.2 = (f32[8]{0:T(128)}, f32[8]{0:T(128)S(1)}, u32[]{:S(2)}) copy-start(f32[8]{0:T(128)S(1)} %psum.22) | copy-start | bytes 100
Sparse Core Ops, SparseCore 0:
  14.3 126.6 all-reduce.1
where the time goes:
time: 363 us; the launch traced here: 362 us
  blocking collectives  204 us (56%)
  waiting for transfers between devices  126 us (35%)
  between operations  16.2 us (4%)
  matrix products  6.72 us (2%)
  other arithmetic  6.38 us (2%)
    psum x1, waiting for transfers between devices, shards(): whole = lax.psum(partial_all, 'ops')  126 us
    psum x1, blocking collectives, shards(): correlations = lax.psum(local_over, ('ops', 'sec'))  105 us
    psum x1, blocking collectives, shards(): total = lax.psum(jnp.sum(resid * resid), ('ops', 'sec'))  99.5 us
  transfers between devices with their start and end apart: 1, of which 1 were waited for; matrix products, arithmetic and copies ran while one was open for 0% of the time, Pallas kernels for 0%

commit v1 on v0

--- a/solution.py
+++ b/solution.py
@@ -5,6 +5,16 @@
 
 
 def shards(wave, left_ops, right_ops, priors, row_sizes, col_sizes):
+
+    def turn_keys(local_x):
+        item_now = local_x
+        parts_n = jax.lax.axis_size("ops")
+        for ii in [kk for kk in (1, 2, 4, 8, 16) if kk < parts_n]:
+            item_now = item_now + jax.lax.ppermute(
+                item_now, "ops", perm=tuple(((p, p ^ ii) for p in range(parts_n)))
+            )
+        return item_now
+
     width = wave.shape[1]
     sec_local = wave.shape[0]
     shard_rows = width // lax.axis_size("ops")
@@ -18,7 +28,7 @@
         "sab,ksjb->ksaj", masked, right_ops, preferred_element_type=jnp.float32
     ).astype(jnp.bfloat16)
     partial_all = jnp.einsum("ksia,ksaj->sij", left_ops, inner, preferred_element_type=jnp.float32)
-    whole = lax.psum(partial_all, "ops")
+    whole = turn_keys(partial_all)
     summed = lax.dynamic_slice_in_dim(whole, first_row, shard_rows, 1)
     mine_rows = lax.dynamic_slice_in_dim(row_mask, first_row, shard_rows, 1)
     mine_mask = mine_rows[:, :, None] * col_mask[:, None, :]

time: 363 us -> 441 us (1.21)
  waiting for transfers between devices: 126 us -> 193 us
  starting transfers between devices: 0.04 us -> 21.1 us
  between operations: 16.2 us -> 2.84 us
  blocking collectives: 204 us -> 211 us
    ppermute x0 -> x4, waiting for transfers between devices: none -> 193 us  [turn_keys(): jax.lax.ppermute(item_now, 'ops', perm=tuple(((p, p ^ ii) for p in range(...]
    psum x1 -> x0, waiting for transfers between devices: 126 us -> none  [shards(): whole = lax.psum(partial_all, 'ops')]
    ppermute x0 -> x4, starting transfers between devices: none -> 21.1 us  [turn_keys(): jax.lax.ppermute(item_now, 'ops', perm=tuple(((p, p ^ ii) for p in range(...]
    psum x1, blocking collectives: 105 us -> 111 us  [shards(): correlations = lax.psum(local_over, ('ops', 'sec'))]
  transfers between devices with their start and end apart: 1 -> 4, of which waited for: 1 -> 4; matrix products, arithmetic and copies ran while one was open for 0% -> 0% of each run, Pallas kernels for 0% -> 0%
where the time goes in v1:
time: 441 us; the launch traced here: 440 us
  blocking collectives  211 us (48%)
  waiting for transfers between devices  193 us (44%)
  starting transfers between devices  21.1 us (5%)
  other arithmetic  6.16 us (1%)
  matrix products  5.88 us (1%)
    ppermute x4, waiting for transfers between devices, turn_keys(): jax.lax.ppermute(item_now, 'ops', perm=tuple(((p, p ^ ii) for p in range(...  193 us
    psum x1, blocking collectives, shards(): correlations = lax.psum(local_over, ('ops', 'sec'))  111 us
    psum x1, blocking collectives, shards(): total = lax.psum(jnp.sum(resid * resid), ('ops', 'sec'))  99.3 us
    ppermute x4, starting transfers between devices, turn_keys(): jax.lax.ppermute(item_now, 'ops', perm=tuple(((p, p ^ ii) for p in range(...  21.1 us
  transfers between devices with their start and end apart: 4, of which 4 were waited for; matrix products, arithmetic and copies ran while one was open for 0% of the time, Pallas kernels for 0%

profile of v1, /device:TPU:1, one launch (start us, length us, event | category | flops | bytes accessed | tf_op | source)
XLA Modules:
  0.0 440.2 jit_solution(13895180917017884375)
XLA Ops:
  0.6 0.0 copy-start
  2.0 0.0 copy-done
  2.1 3.7 convolution_bitcast_fusion
  5.7 4.0 collective-permute-start
  9.8 46.1 %collective-permute-done = f32[1,768,768]{2,1,0:T(8,128)S(1)} collective-permute-done((f32[1,768,768]{2,1,0:T(8,128)S(1)}, f32[1,768,768]{2,1,0:T(8,128)S(1)}, u32[]{:S(2)}, u32[]{:S(2)}) %collective-permute-start) | collective-permute-done | bytes 2359328 | tf_op jit(solution)/shard_map/ppermute | solution.py:13
  55.9 0.3 add.23
  56.2 9.5 %collective-permute-start.1 = (f32[1,768,768]{2,1,0:T(8,128)S(1)}, f32[1,768,768]{2,1,0:T(8,128)S(1)}, u32[]{:S(2)}, u32[]{:S(2)}) collective-permute-start(f32[1,768,768]{2,1,0:T(8,128)S(1)} %add.23), channel_id=1, source_target_pairs={{0,64},{32,96},{64,0},{96,32},{128,192},{160,224},{192,128},{224,1... | collective-permute-start | bytes 7077896 | tf_op jit(solution)/shard_map/ppermute | solution.py:13
  65.7 49.9 %collective-permute-done.1 = f32[1,768,768]{2,1,0:T(8,128)S(1)} collective-permute-done((f32[1,768,768]{2,1,0:T(8,128)S(1)}, f32[1,768,768]{2,1,0:T(8,128)S(1)}, u32[]{:S(2)}, u32[]{:S(2)}) %collective-permute-start.1) | collective-permute-done | bytes 2359328 | tf_op jit(solution)/shard_map/ppermute | solution.py:13
  115.6 0.3 add.24
  115.9 3.1 collective-permute-start.2
  119.0 49.4 %collective-permute-done.2 = f32[1,768,768]{2,1,0:T(8,128)S(1)} collective-permute-done((f32[1,768,768]{2,1,0:T(8,128)S(1)}, f32[1,768,768]{2,1,0:T(8,128)S(1)}, u32[]{:S(2)}, u32[]{:S(2)}) %collective-permute-start.2) | collective-permute-done | bytes 2359328 | tf_op jit(solution)/shard_map/ppermute | solution.py:13
  168.4 0.3 add.25
  168.7 4.5 %collective-permute-start.3 = (f32[1,768,768]{2,1,0:T(8,128)S(1)}, f32[1,768,768]{2,1,0:T(8,128)}, u32[]{:S(2)}, u32[]{:S(2)}) collective-permute-start(f32[1,768,768]{2,1,0:T(8,128)S(1)} %add.25), channel_id=1, source_target_pairs={{0,256},{32,288},{64,320},{96,352},{128,384},{160,416},{192,448},{... | collective-permute-start | bytes 7077896 | tf_op jit(solution)/shard_map/ppermute | solution.py:13
  173.2 0.1 multiply_convert_fusion.1
  173.2 1.1 multiply_bitcast_fusion
  174.4 0.0 copy-start.1
  174.4 47.5 %collective-permute-done.3 = f32[1,768,768]{2,1,0:T(8,128)} collective-permute-done((f32[1,768,768]{2,1,0:T(8,128)S(1)}, f32[1,768,768]{2,1,0:T(8,128)}, u32[]{:S(2)}, u32[]{:S(2)}) %collective-permute-start.3) | collective-permute-done | bytes 2359328 | tf_op jit(solution)/shard_map/ppermute | solution.py:13
  221.8 1.0 fusion.15
  222.8 0.0 copy-start.2
  222.8 0.0 copy-done.1
  222.9 0.6 copy-done.2
  223.5 0.5 convolution_bitcast_fusion.1
  224.0 111.4 %psum.14 = f32[8]{0:T(128)S(1)} all-reduce(f32[8]{0:T(128)S(1)} %convolution_bitcast_fusion.1), channel_id=1, replica_groups=mesh['ops'=16,'sec'=32] {'ops','sec'}, use_global_device_ids=true, to_apply=%region_0.0 | all-reduce | flops 8 | bytes 64 | tf_op jit(solution)/shard_map/psum | solution.py:39
  335.4 0.0 copy-start.3
  335.4 1.7 fusion.11
  337.1 1.5 multiply_reduce_fusion
  338.7 99.3 %psum.15 = f32[]{:T(128)} all-reduce(f32[]{:T(128)} %multiply_reduce_fusion), channel_id=1, replica_groups=mesh['ops'=16,'sec'=32] {'ops','sec'}, use_global_device_ids=true, to_apply=%region_2.0 | all-reduce | flops 1 | bytes 8 | tf_op jit(solution)/shard_map/psum | solution.py:41
  438.7 1.5 divide_convert_fusion
  440.2 0.0 copy-done.3
  (2 shorter events, 0.0 us)
Async XLA Ops:
  0.6 1.4 copy-start
  5.7 50.2 %collective-permute-start = (f32[1,768,768]{2,1,0:T(8,128)S(1)}, f32[1,768,768]{2,1,0:T(8,128)S(1)}, u32[]{:S(2)}, u32[]{:S(2)}) collective-permute-start(f32[1,768,768]{2,1,0:T(8,128)S(1)} %convolution_bitcast_fusion), channel_id=1, source_target_pairs={{0,32},{32,0},{64,96},{96,64},{128,160},{160,128},{192,224},{224,1... | collective-permute-start | bytes 7077896 | tf_op jit(solution)/shard_map/ppermute | solution.py:13
  56.2 59.4 %collective-permute-start.1 = (f32[1,768,768]{2,1,0:T(8,128)S(1)}, f32[1,768,768]{2,1,0:T(8,128)S(1)}, u32[]{:S(2)}, u32[]{:S(2)}) collective-permute-start(f32[1,768,768]{2,1,0:T(8,128)S(1)} %add.23), channel_id=1, source_target_pairs={{0,64},{32,96},{64,0},{96,32},{128,192},{160,224},{192,128},{224,1... | collective-permute-start | bytes 7077896 | tf_op jit(solution)/shard_map/ppermute | solution.py:13
  115.9 52.4 %collective-permute-start.2 = (f32[1,768,768]{2,1,0:T(8,128)S(1)}, f32[1,768,768]{2,1,0:T(8,128)S(1)}, u32[]{:S(2)}, u32[]{:S(2)}) collective-permute-start(f32[1,768,768]{2,1,0:T(8,128)S(1)} %add.24), channel_id=1, source_target_pairs={{0,128},{32,160},{64,192},{96,224},{128,0},{160,32},{192,64},{224,... | collective-permute-start | bytes 7077896 | tf_op jit(solution)/shard_map/ppermute | solution.py:13
  168.7 53.2 %collective-permute-start.3 = (f32[1,768,768]{2,1,0:T(8,128)S(1)}, f32[1,768,768]{2,1,0:T(8,128)}, u32[]{:S(2)}, u32[]{:S(2)}) collective-permute-start(f32[1,768,768]{2,1,0:T(8,128)S(1)} %add.25), channel_id=1, source_target_pairs={{0,256},{32,288},{64,320},{96,352},{128,384},{160,416},{192,448},{... | collective-permute-start | bytes 7077896 | tf_op jit(solution)/shard_map/ppermute | solution.py:13
  174.4 48.5 %copy-start.1 = (bf16[8,48,768]{2,1,0:T(8,128)(2,1)}, bf16[8,48,768]{2,1,0:T(8,128)(2,1)S(1)}, u32[]{:S(2)}) copy-start(bf16[8,48,768]{2,1,0:T(8,128)(2,1)S(1)} %multiply_bitcast_fusion) | copy-start | bytes 1769476
  222.8 0.6 copy-start.2
  335.4 104.8 %copy-start.3 = (f32[8]{0:T(128)}, f32[8]{0:T(128)S(1)}, u32[]{:S(2)}) copy-start(f32[8]{0:T(128)S(1)} %psum.14) | copy-start | bytes 100
